TPU v7x, 32 devices: a whole 2x2x4 slice. The times are simulated.
32 devices in a mesh: wave: 4 (over y, core), lev: 4 (over z), cpl: 2 (over x).
Axes of the slice: x: 2, y: 2, z: 4, core: 2. Of those that a mesh axis runs over, the one named last changes fastest.
Arguments:
- spectral: bfloat16 [1280, 2, 4, 24, 1280], P('wave', None, None, 'lev'), may hold values from -0.125 to 0.125
- legendre: bfloat16 [1280, 16, 1280], P('wave', 'cpl'), may hold values from -0.15625 to 0.15625
- wavenumber: int32 [1280], replicated, may hold values from 0 to 1279, each once
- level_weight: float32 [24], P('lev'), may hold values from 0.1 to 1
- source_row: int32 [16], replicated, may hold values from 0 to 14
- row_weight: float32 [16], replicated, may hold values from 0.2 to 0.8
Outputs:
- ocean_flux: float32 [16, 4, 4320], P(('wave', 'cpl'), None, 'lev')
All inputs are finite; a program needn't handle non-finite values.
Results may differ from a plain program's by a relative error of at most 0.0041.
Values may be sent and summed in bfloat16 or wider, within the bound.
No kernel may reach another device: no remote copies, remote signals or barrier semaphores. Data moves between devices by JAX's collectives and lax.ppermute only.
A program may use at most 192 MiB of HBM per device.

v0:
```python
import math
import jax
import jax.numpy as jnp
from jax import lax
from jax.sharding import PartitionSpec as P

NLON = 4320


def phase_angle(phase, lon_total):
    return phase.astype(jnp.float32) * (2.0 * math.pi / lon_total)


def surface_flux(grid_vals, level_weight):
    wind_speed = jnp.sqrt(grid_vals[..., 0, :, :] ** 2 + grid_vals[..., 1, :, :] ** 2 + 0.25)
    return jnp.sum(level_weight[:, None] * wind_speed[..., None, :, :] * grid_vals, axis=-2)


def latitude_order(gathered, wave_count, cpl_count, lat_dev):
    trailing = gathered.shape[1:]
    gathered = gathered.reshape((wave_count, cpl_count, lat_dev) + trailing)
    gathered = jnp.swapaxes(gathered, 0, 1)
    return gathered.reshape((wave_count * cpl_count * lat_dev,) + trailing)


def interpolate(gathered, source, weight_hi):
    lower = jnp.take(gathered, source, axis=0)
    upper = jnp.take(gathered, source + 1, axis=0)
    return (1.0 - weight_hi[:, None, None]) * lower + weight_hi[:, None, None] * upper


def local(spectral, legendre, wavenumber, level_weight, source_row, row_weight):
    slot_count = spectral.shape[0]
    fields = spectral.shape[2]
    levels = spectral.shape[3]
    degree = spectral.shape[4]
    channels = 2 * fields * levels
    wave_count = lax.axis_size("wave")
    cpl_count = lax.axis_size("cpl")
    wave_at = lax.axis_index("wave")
    cpl_at = lax.axis_index("cpl")
    owned_waves = lax.dynamic_slice_in_dim(wavenumber, wave_at * slot_count, slot_count)
    coefficient = spectral.reshape(slot_count, channels, degree)
    in_triangle = (
        lax.broadcasted_iota(jnp.int32, (slot_count, 1, degree), 2)
        < (degree - owned_waves)[:, None, None]
    )
    coefficient = jnp.where(in_triangle, coefficient, jnp.zeros_like(coefficient))
    spec_grid = jnp.einsum(
        "skj,slj->slk", coefficient, legendre, preferred_element_type=jnp.float32
    ).astype(jnp.bfloat16)
    by_latitude = lax.all_to_all(spec_grid, "wave", split_axis=1, concat_axis=0, tiled=True)
    total_slots = by_latitude.shape[0]
    lat_dev = by_latitude.shape[1]
    rows_in = (
        by_latitude.reshape(total_slots, lat_dev, 2, fields * levels)
        .transpose(1, 3, 0, 2)
        .reshape(lat_dev * fields * levels, 2 * total_slots)
    )
    lon_block = NLON // 8
    factor = jnp.where(wavenumber == 0, 1.0, 2.0).astype(jnp.float32)[:, None]
    offsets = jnp.arange(lon_block, dtype=jnp.int32)
    base_angle = phase_angle(wavenumber[:, None] * offsets[None, :] % NLON, NLON)
    base_cos = jnp.cos(base_angle)
    base_sin = jnp.sin(base_angle)

    def one_block(first_lon):
        start_angle = phase_angle(wavenumber * first_lon % NLON, NLON)[:, None]
        start_cos = jnp.cos(start_angle)
        start_sin = jnp.sin(start_angle)
        cos_vals = start_cos * base_cos - start_sin * base_sin
        sin_vals = start_sin * base_cos + start_cos * base_sin
        fourier = (
            jnp.stack([factor * cos_vals, -factor * sin_vals], axis=1)
            .astype(jnp.bfloat16)
            .reshape(2 * total_slots, lon_block)
        )
        grid_vals = jnp.dot(rows_in, fourier, preferred_element_type=jnp.float32).reshape(
            lat_dev, fields, levels, lon_block
        )
        return surface_flux(grid_vals, level_weight)

    block_starts = jnp.arange(8, dtype=jnp.int32) * lon_block
    per_block = lax.map(one_block, block_starts)
    partial_value = per_block.transpose(1, 2, 0, 3).reshape(lat_dev, fields, NLON)
    own_first = (wave_at * cpl_count + cpl_at) * lat_dev
    source = lax.dynamic_slice_in_dim(source_row, own_first, lat_dev)
    weight_hi = lax.dynamic_slice_in_dim(row_weight, own_first, lat_dev)
    strip_width = NLON // lax.axis_size("lev")
    summed = lax.psum(partial_value, "lev")
    gathered = lax.all_gather(summed, ("wave", "cpl"), axis=0, tiled=True)
    gathered = latitude_order(gathered, wave_count, cpl_count, lat_dev)
    gathered = lax.dynamic_slice_in_dim(
        gathered, lax.axis_index("lev") * strip_width, strip_width, 2
    )
    return interpolate(gathered, source, weight_hi)


def solution(mesh):
    placed = (P("wave", None, None, "lev", None), P("wave", "cpl", None), P(), P("lev"), P(), P())
    return jax.shard_map(
        local,
        mesh=mesh,
        in_specs=placed,
        out_specs=P(("wave", "cpl"), None, "lev"),
        check_vma=False,
    )
```

profile of v0, /device:TPU:0, one launch (start us, length us, event | category | flops | bytes accessed | tf_op | source)
XLA Modules:
  0.0 437.1 jit_solution(12876540771261802303)
XLA Ops:
  7.6 26.6 %copy.16 = bf16[320,2,4,6,1280]{4,0,3,2,1:T(8,128)(2,1)} copy(bf16[320,2,4,6,1280]{4,2,3,1,0:T(4,128)(2,1)} %param.10) | data formatting | bytes 78643200 | tf_op args[0]
  34.2 26.6 %bitcast_select_fusion = bf16[320,48,1280]{2,0,1:T(8,128)(2,1)} fusion(bf16[320,2,4,6,1280]{4,0,3,2,1:T(8,128)(2,1)} %copy.16, pred[320,1280]{1,0:T(8,128)(4,1)S(1)} %iota_compare_fusion), kind=kLoop, calls=%fused_computation.40 | loop fusion | flops 19660800 | bytes 79052800 | tf_op jit(solution)/shard_map/jit(_where)/select_n | solution.py:48
  60.8 47.0 %fusion.31 = bf16[320,8,48]{2,1,0:T(8,128)(2,1)S(1)} fusion(bf16[320,8,1280]{2,1,0:T(8,128)(2,1)} %param.11, bf16[320,48,1280]{2,0,1:T(8,128)(2,1)} %bitcast_select_fusion), kind=kOutput, calls=%fused_computation.45 | convolution fusion | flops 314695680 | bytes 46120960 | tf_op jit(solution)/shard_map/skj,slj->slk/dot_general | solution.py:49
  109.0 4.2 all-to-all-start
  113.3 6.3 %all-to-all-done = bf16[320,8,48]{0,2,1:T(8,128)(2,1)S(1)} async-done(((bf16[320,8,48]{0,2,1:T(8,128)(2,1)}), bf16[320,8,48]{0,2,1:T(8,128)(2,1)S(1)}, u32[]{:S(2)}, u32[]{:S(2)}) %all-to-all-start) | async-done | bytes 245792 | tf_op jit(solution)/shard_map/all_to_all | solution.py:52
  123.3 240.5 %while.14 = (s32[]{:T(128)}, f32[8,2,4,540]{3,2,1,0:T(4,128)}, f32[6]{0:T(128)S(1)}, f32[1280,1]{0,1:T(1,128)S(1)}, s32[8]{0:T(128)S(1)}, /*index=5*/s32[1280]{0...) while((s32[]{:T(128)}, f32[8,2,4,540]{3,2,1,0:T(4,128)}, ...), condition=%wide.region_2.3_spmd.clone.clone, body=%wide.region_0.2_spmd.clone.clone.sunk | while | flops 147317040 | bytes 22999700 | solution.py:84
  124.5 12.4 %fusion.47 = (bf16[1280,1,540]{0,2,1:T(8,128)(2,1)S(1)}, bf16[1280,1,540]{0,2,1:T(8,128)(2,1)S(1)}) fusion(s32[1280]{0:T(1024)S(1)} %get-tuple-element.302, f32[1280]{0:T(1024)S(1)} %get-tuple-element.273, f32[1280]{0:T(1024)S(1)} %get-tuple-element.274, f32[1280]{0:T(1024)S(1)} %reduce.4, f32[1280]{0:T(1024)S(1)} %reduce.5), kind=kLoop, calls=%fused_computation.12.clone.1 | loop fusion | flops 13132800 | bytes 2790400 | tf_op jit(solution)/shard_map/convert
  137.2 7.2 %copy.33 = bf16[1280,2,540]{2,1,0:T(2,128)(2,1)} copy(bf16[1280,2,540]{0,2,1:T(8,128)(2,1)S(1)} %pad_maximum_fusion.2) | data formatting | bytes 5529600 | tf_op jit(solution)/shard_map/while/body/eval_jaxpr/stack | solution.py:74
  144.4 6.6 %convert_element_type.80 = bf16[2560,540]{1,0:T(8,128)(2,1)S(1)} reshape(bf16[1280,2,540]{2,1,0:T(2,128)(2,1)} %copy.33) | data formatting | bytes 5529600 | tf_op jit(solution)/shard_map/while/body/eval_jaxpr/convert_element_type | solution.py:75
  154.6 12.4 %fusion.47 = (bf16[1280,1,540]{0,2,1:T(8,128)(2,1)S(1)}, bf16[1280,1,540]{0,2,1:T(8,128)(2,1)S(1)}) fusion(s32[1280]{0:T(1024)S(1)} %get-tuple-element.302, f32[1280]{0:T(1024)S(1)} %get-tuple-element.273, f32[1280]{0:T(1024)S(1)} %get-tuple-element.274, f32[1280]{0:T(1024)S(1)} %reduce.4, f32[1280]{0:T(1024)S(1)} %reduce.5), kind=kLoop, calls=%fused_computation.12.clone.1 | loop fusion | flops 13132800 | bytes 2790400 | tf_op jit(solution)/shard_map/convert
  167.3 7.2 %copy.33 = bf16[1280,2,540]{2,1,0:T(2,128)(2,1)} copy(bf16[1280,2,540]{0,2,1:T(8,128)(2,1)S(1)} %pad_maximum_fusion.2) | data formatting | bytes 5529600 | tf_op jit(solution)/shard_map/while/body/eval_jaxpr/stack | solution.py:74
  174.5 6.6 %convert_element_type.80 = bf16[2560,540]{1,0:T(8,128)(2,1)S(1)} reshape(bf16[1280,2,540]{2,1,0:T(2,128)(2,1)} %copy.33) | data formatting | bytes 5529600 | tf_op jit(solution)/shard_map/while/body/eval_jaxpr/convert_element_type | solution.py:75
  184.7 12.4 %fusion.47 = (bf16[1280,1,540]{0,2,1:T(8,128)(2,1)S(1)}, bf16[1280,1,540]{0,2,1:T(8,128)(2,1)S(1)}) fusion(s32[1280]{0:T(1024)S(1)} %get-tuple-element.302, f32[1280]{0:T(1024)S(1)} %get-tuple-element.273, f32[1280]{0:T(1024)S(1)} %get-tuple-element.274, f32[1280]{0:T(1024)S(1)} %reduce.4, f32[1280]{0:T(1024)S(1)} %reduce.5), kind=kLoop, calls=%fused_computation.12.clone.1 | loop fusion | flops 13132800 | bytes 2790400 | tf_op jit(solution)/shard_map/convert
  197.3 7.2 %copy.33 = bf16[1280,2,540]{2,1,0:T(2,128)(2,1)} copy(bf16[1280,2,540]{0,2,1:T(8,128)(2,1)S(1)} %pad_maximum_fusion.2) | data formatting | bytes 5529600 | tf_op jit(solution)/shard_map/while/body/eval_jaxpr/stack | solution.py:74
  204.5 6.6 %convert_element_type.80 = bf16[2560,540]{1,0:T(8,128)(2,1)S(1)} reshape(bf16[1280,2,540]{2,1,0:T(2,128)(2,1)} %copy.33) | data formatting | bytes 5529600 | tf_op jit(solution)/shard_map/while/body/eval_jaxpr/convert_element_type | solution.py:75
  214.7 12.4 %fusion.47 = (bf16[1280,1,540]{0,2,1:T(8,128)(2,1)S(1)}, bf16[1280,1,540]{0,2,1:T(8,128)(2,1)S(1)}) fusion(s32[1280]{0:T(1024)S(1)} %get-tuple-element.302, f32[1280]{0:T(1024)S(1)} %get-tuple-element.273, f32[1280]{0:T(1024)S(1)} %get-tuple-element.274, f32[1280]{0:T(1024)S(1)} %reduce.4, f32[1280]{0:T(1024)S(1)} %reduce.5), kind=kLoop, calls=%fused_computation.12.clone.1 | loop fusion | flops 13132800 | bytes 2790400 | tf_op jit(solution)/shard_map/convert
  227.4 7.2 %copy.33 = bf16[1280,2,540]{2,1,0:T(2,128)(2,1)} copy(bf16[1280,2,540]{0,2,1:T(8,128)(2,1)S(1)} %pad_maximum_fusion.2) | data formatting | bytes 5529600 | tf_op jit(solution)/shard_map/while/body/eval_jaxpr/stack | solution.py:74
  234.6 6.6 %convert_element_type.80 = bf16[2560,540]{1,0:T(8,128)(2,1)S(1)} reshape(bf16[1280,2,540]{2,1,0:T(2,128)(2,1)} %copy.33) | data formatting | bytes 5529600 | tf_op jit(solution)/shard_map/while/body/eval_jaxpr/convert_element_type | solution.py:75
  244.8 12.4 %fusion.47 = (bf16[1280,1,540]{0,2,1:T(8,128)(2,1)S(1)}, bf16[1280,1,540]{0,2,1:T(8,128)(2,1)S(1)}) fusion(s32[1280]{0:T(1024)S(1)} %get-tuple-element.302, f32[1280]{0:T(1024)S(1)} %get-tuple-element.273, f32[1280]{0:T(1024)S(1)} %get-tuple-element.274, f32[1280]{0:T(1024)S(1)} %reduce.4, f32[1280]{0:T(1024)S(1)} %reduce.5), kind=kLoop, calls=%fused_computation.12.clone.1 | loop fusion | flops 13132800 | bytes 2790400 | tf_op jit(solution)/shard_map/convert
  257.5 7.2 %copy.33 = bf16[1280,2,540]{2,1,0:T(2,128)(2,1)} copy(bf16[1280,2,540]{0,2,1:T(8,128)(2,1)S(1)} %pad_maximum_fusion.2) | data formatting | bytes 5529600 | tf_op jit(solution)/shard_map/while/body/eval_jaxpr/stack | solution.py:74
  264.7 6.6 %convert_element_type.80 = bf16[2560,540]{1,0:T(8,128)(2,1)S(1)} reshape(bf16[1280,2,540]{2,1,0:T(2,128)(2,1)} %copy.33) | data formatting | bytes 5529600 | tf_op jit(solution)/shard_map/while/body/eval_jaxpr/convert_element_type | solution.py:75
  274.9 12.4 %fusion.47 = (bf16[1280,1,540]{0,2,1:T(8,128)(2,1)S(1)}, bf16[1280,1,540]{0,2,1:T(8,128)(2,1)S(1)}) fusion(s32[1280]{0:T(1024)S(1)} %get-tuple-element.302, f32[1280]{0:T(1024)S(1)} %get-tuple-element.273, f32[1280]{0:T(1024)S(1)} %get-tuple-element.274, f32[1280]{0:T(1024)S(1)} %reduce.4, f32[1280]{0:T(1024)S(1)} %reduce.5), kind=kLoop, calls=%fused_computation.12.clone.1 | loop fusion | flops 13132800 | bytes 2790400 | tf_op jit(solution)/shard_map/convert
  287.5 7.2 %copy.33 = bf16[1280,2,540]{2,1,0:T(2,128)(2,1)} copy(bf16[1280,2,540]{0,2,1:T(8,128)(2,1)S(1)} %pad_maximum_fusion.2) | data formatting | bytes 5529600 | tf_op jit(solution)/shard_map/while/body/eval_jaxpr/stack | solution.py:74
  294.7 6.6 %convert_element_type.80 = bf16[2560,540]{1,0:T(8,128)(2,1)S(1)} reshape(bf16[1280,2,540]{2,1,0:T(2,128)(2,1)} %copy.33) | data formatting | bytes 5529600 | tf_op jit(solution)/shard_map/while/body/eval_jaxpr/convert_element_type | solution.py:75
  304.9 12.4 %fusion.47 = (bf16[1280,1,540]{0,2,1:T(8,128)(2,1)S(1)}, bf16[1280,1,540]{0,2,1:T(8,128)(2,1)S(1)}) fusion(s32[1280]{0:T(1024)S(1)} %get-tuple-element.302, f32[1280]{0:T(1024)S(1)} %get-tuple-element.273, f32[1280]{0:T(1024)S(1)} %get-tuple-element.274, f32[1280]{0:T(1024)S(1)} %reduce.4, f32[1280]{0:T(1024)S(1)} %reduce.5), kind=kLoop, calls=%fused_computation.12.clone.1 | loop fusion | flops 13132800 | bytes 2790400 | tf_op jit(solution)/shard_map/convert
  317.6 7.2 %copy.33 = bf16[1280,2,540]{2,1,0:T(2,128)(2,1)} copy(bf16[1280,2,540]{0,2,1:T(8,128)(2,1)S(1)} %pad_maximum_fusion.2) | data formatting | bytes 5529600 | tf_op jit(solution)/shard_map/while/body/eval_jaxpr/stack | solution.py:74
  324.8 6.6 %convert_element_type.80 = bf16[2560,540]{1,0:T(8,128)(2,1)S(1)} reshape(bf16[1280,2,540]{2,1,0:T(2,128)(2,1)} %copy.33) | data formatting | bytes 5529600 | tf_op jit(solution)/shard_map/while/body/eval_jaxpr/convert_element_type | solution.py:75
  335.0 12.4 %fusion.47 = (bf16[1280,1,540]{0,2,1:T(8,128)(2,1)S(1)}, bf16[1280,1,540]{0,2,1:T(8,128)(2,1)S(1)}) fusion(s32[1280]{0:T(1024)S(1)} %get-tuple-element.302, f32[1280]{0:T(1024)S(1)} %get-tuple-element.273, f32[1280]{0:T(1024)S(1)} %get-tuple-element.274, f32[1280]{0:T(1024)S(1)} %reduce.4, f32[1280]{0:T(1024)S(1)} %reduce.5), kind=kLoop, calls=%fused_computation.12.clone.1 | loop fusion | flops 13132800 | bytes 2790400 | tf_op jit(solution)/shard_map/convert
  347.7 7.2 %copy.33 = bf16[1280,2,540]{2,1,0:T(2,128)(2,1)} copy(bf16[1280,2,540]{0,2,1:T(8,128)(2,1)S(1)} %pad_maximum_fusion.2) | data formatting | bytes 5529600 | tf_op jit(solution)/shard_map/while/body/eval_jaxpr/stack | solution.py:74
  354.9 6.6 %convert_element_type.80 = bf16[2560,540]{1,0:T(8,128)(2,1)S(1)} reshape(bf16[1280,2,540]{2,1,0:T(2,128)(2,1)} %copy.33) | data formatting | bytes 5529600 | tf_op jit(solution)/shard_map/while/body/eval_jaxpr/convert_element_type | solution.py:75
  365.6 35.4 %all-reduce.2.cloned.1.call-done = f32[2,4,4320]{2,1,0:T(4,128)} async-done(((f32[2,4,4320]{2,1,0:T(4,128)}), f32[2,4,4320]{2,1,0:T(4,128)}) %all-reduce.2.cloned.1.call-update) | async-done | bytes 138256 | tf_op jit(solution)/shard_map/psum | solution.py:90
  401.2 25.6 %all-gather.2.cloned.1.call-done = f32[16,4,4320]{2,1,0:T(4,128)} async-done(((f32[2,4,4320]{2,1,0:T(4,128)}), f32[16,4,4320]{2,1,0:T(4,128)}) %all-gather.2.cloned.1.call-update) | async-done | bytes 1105936 | tf_op jit(solution)/shard_map/all_gather | solution.py:91
  (115 shorter events, 41.6 us)
Async XLA Ops:
  60.8 52.4 %copy-start = (s32[1280]{0:T(1024)S(1)}, s32[1280]{0:T(1024)}, u32[]{:S(2)}) copy-start(s32[1280]{0:T(1024)} %param.12) | copy-start | bytes 15364
  109.0 10.6 %all-to-all-start = ((bf16[320,8,48]{0,2,1:T(8,128)(2,1)}), bf16[320,8,48]{0,2,1:T(8,128)(2,1)S(1)}, u32[]{:S(2)}, u32[]{:S(2)}) async-start(bf16[320,8,48]{0,2,1:T(8,128)(2,1)} %copy.18), calls=%async_computation | async-start | bytes 589824 | tf_op jit(solution)/shard_map/all_to_all | solution.py:52
  113.2 287.8 %all-reduce.2.cloned.1.call-start = ((), (), s32[]{:S(2)}) async-start(), calls=%async_computation.1 | async-start | bytes 278528 | tf_op jit(solution)/shard_map/psum | solution.py:90
  113.2 10.0 %copy-start.1 = (f32[6]{0:T(128)S(1)}, f32[6]{0:T(128)}, u32[]{:S(2)}) copy-start(f32[6]{0:T(128)} %param.13) | copy-start | bytes 76
  123.3 277.8 %copy-start.2 = (f32[16]{0:T(128)S(1)}, f32[16]{0:T(128)}, u32[]{:S(2)}) copy-start(f32[16]{0:T(128)} %param.15) | copy-start | bytes 196
  123.3 277.9 %copy-start.3 = (s32[16]{0:T(128)S(1)}, s32[16]{0:T(128)}, u32[]{:S(2)}) copy-start(s32[16]{0:T(128)} %param.14) | copy-start | bytes 196
  365.6 61.3 %all-gather.2.cloned.1.call-start = ((), (), s32[]{:S(2)}) async-start(), calls=%async_computation.2 | async-start | bytes 1253376 | tf_op jit(solution)/shard_map/all_gather | solution.py:91
Sparse Core Ops, SparseCore 0:
  365.7 35.2 all-reduce.1
  403.0 23.7 all-gather.1
where the time goes:
time: 439 us; the launch traced here: 437 us
  local copies, waits for them, and re-layouts  156 us (36%)
  other arithmetic  136 us (31%)
  waiting for transfers between devices  67.4 us (15%)
  matrix products  59.3 us (14%)
  between operations  13.5 us (3%)
    another operation x24, other arithmetic  99.7 us
    another operation x8, local copies, waits for them, and re-layouts, one_block(): jnp.stack([factor * cos_vals, -factor * sin_vals], axis=1)  57.6 us
    convert_element_type x8, local copies, waits for them, and re-layouts, one_block(): fourier = jnp.stack([factor * cos_vals, -factor * sin_vals], axis=1).asty...  52.9 us
    dot_general x1, matrix products, local(): jnp.einsum('skj,slj->slk', coefficient, legendre, preferred_element_type=...  47 us
    psum x1, waiting for transfers between devices, local(): summed = lax.psum(partial_value, 'lev')  35.4 us
    unnamed x10, local copies, waits for them, and re-layouts  27.6 us
    select_n x1, other arithmetic, local(): jnp.where(in_triangle, coefficient, jnp.zeros_like(coefficient))  26.6 us
    all_gather x1, waiting for transfers between devices, local(): gathered = lax.all_gather(summed, ('wave', 'cpl'), axis=0, tiled=True)  25.6 us
  transfers between devices with their start and end apart: 3, of which 3 were waited for; matrix products, arithmetic and copies ran while one was open for 0% of the time, Pallas kernels for 0%

commit v1 on v0

--- a/solution.py
+++ b/solution.py
@@ -87,7 +87,7 @@
     source = lax.dynamic_slice_in_dim(source_row, own_first, lat_dev)
     weight_hi = lax.dynamic_slice_in_dim(row_weight, own_first, lat_dev)
     strip_width = NLON // lax.axis_size("lev")
-    summed = lax.psum(partial_value, "lev")
+    summed = jnp.sum(lax.all_gather(partial_value, "lev"), axis=0)
     gathered = lax.all_gather(summed, ("wave", "cpl"), axis=0, tiled=True)
     gathered = latitude_order(gathered, wave_count, cpl_count, lat_dev)
     gathered = lax.dynamic_slice_in_dim(

time: 439 us -> 420 us (0.957)
  waiting for transfers between devices: 67.4 us -> 30.9 us
  blocking collectives: 0 us -> 16.6 us
    psum x1 -> x0, waiting for transfers between devices: 35.4 us -> none  [local(): summed = lax.psum(partial_value, 'lev')]
    all_gather x0 -> x1, blocking collectives: none -> 16.6 us  [local(): summed = jnp.sum(lax.all_gather(partial_value, 'lev'), axis=0)]
  transfers between devices with their start and end apart: 3 -> 2, of which waited for: 3 -> 2; matrix products, arithmetic and copies ran while one was open for 0% -> 0% of each run, Pallas kernels for 0% -> 0%
where the time goes in v1:
time: 420 us; the launch traced here: 419 us
  local copies, waits for them, and re-layouts  156 us (37%)
  other arithmetic  138 us (33%)
  matrix products  59.4 us (14%)
  waiting for transfers between devices  30.9 us (7%)
  blocking collectives  16.6 us (4%)
  between operations  13.5 us (3%)
  starting transfers between devices  4.24 us (1%)
    another operation x24, other arithmetic  99.7 us
    another operation x8, local copies, waits for them, and re-layouts, one_block(): jnp.stack([factor * cos_vals, -factor * sin_vals], axis=1)  58.2 us
    convert_element_type x8, local copies, waits for them, and re-layouts, one_block(): fourier = jnp.stack([factor * cos_vals, -factor * sin_vals], axis=1).asty...  52.9 us
    dot_general x1, matrix products, local(): jnp.einsum('skj,slj->slk', coefficient, legendre, preferred_element_type=...  47 us
    unnamed x10, local copies, waits for them, and re-layouts  27.6 us
    select_n x1, other arithmetic, local(): jnp.where(in_triangle, coefficient, jnp.zeros_like(coefficient))  26.6 us
    all_gather x1, waiting for transfers between devices, local(): gathered = lax.all_gather(summed, ('wave', 'cpl'), axis=0, tiled=True)  24.6 us
    all_gather x1, blocking collectives, local(): summed = jnp.sum(lax.all_gather(partial_value, 'lev'), axis=0)  16.6 us
  transfers between devices with their start and end apart: 2, of which 2 were waited for; matrix products, arithmetic and copies ran while one was open for 0% of the time, Pallas kernels for 0%

profile of v1, /device:TPU:0, one launch (start us, length us, event | category | flops | bytes accessed | tf_op | source)
XLA Modules:
  0.0 418.6 jit_solution(6933421772484680530)
XLA Ops:
  7.6 26.6 %copy.23 = bf16[320,2,4,6,1280]{4,0,3,2,1:T(8,128)(2,1)} copy(bf16[320,2,4,6,1280]{4,2,3,1,0:T(4,128)(2,1)} %param.10) | data formatting | bytes 78643200 | tf_op args[0]
  34.2 26.6 %bitcast_select_fusion = bf16[320,48,1280]{2,0,1:T(8,128)(2,1)} fusion(bf16[320,2,4,6,1280]{4,0,3,2,1:T(8,128)(2,1)} %copy.23, pred[320,1280]{1,0:T(8,128)(4,1)S(1)} %iota_compare_fusion), kind=kLoop, calls=%fused_computation.40 | loop fusion | flops 19660800 | bytes 79052800 | tf_op jit(solution)/shard_map/jit(_where)/select_n | solution.py:48
  60.9 47.0 %fusion.31 = bf16[320,8,48]{2,1,0:T(8,128)(2,1)S(1)} fusion(bf16[320,8,1280]{2,1,0:T(8,128)(2,1)} %param.11, bf16[320,48,1280]{2,0,1:T(8,128)(2,1)} %bitcast_select_fusion), kind=kOutput, calls=%fused_computation.45 | convolution fusion | flops 314695680 | bytes 46120960 | tf_op jit(solution)/shard_map/skj,slj->slk/dot_general | solution.py:49
  109.0 4.2 %all-to-all-start = ((bf16[320,8,48]{0,2,1:T(8,128)(2,1)}), bf16[320,8,48]{0,2,1:T(8,128)(2,1)S(1)}, u32[]{:S(2)}, u32[]{:S(2)}) async-start(bf16[320,8,48]{0,2,1:T(8,128)(2,1)} %copy.25), calls=%async_computation | async-start | bytes 589824 | tf_op jit(solution)/shard_map/all_to_all | solution.py:52
  113.4 6.3 %all-to-all-done = bf16[320,8,48]{0,2,1:T(8,128)(2,1)S(1)} async-done(((bf16[320,8,48]{0,2,1:T(8,128)(2,1)}), bf16[320,8,48]{0,2,1:T(8,128)(2,1)S(1)}, u32[]{:S(2)}, u32[]{:S(2)}) %all-to-all-start) | async-done | bytes 245792 | tf_op jit(solution)/shard_map/all_to_all | solution.py:52
  123.4 241.7 %while.14 = (s32[]{:T(128)}, f32[8,2,4,540]{3,2,1,0:T(4,128)}, f32[6]{0:T(128)S(1)}, f32[1280,1]{0,1:T(1,128)S(1)}, s32[8]{0:T(128)S(1)}, /*index=5*/s32[1280]{0...) while((s32[]{:T(128)}, f32[8,2,4,540]{3,2,1,0:T(4,128)}, ...), condition=%wide.region_2.3_spmd.clone.clone, body=%wide.region_0.2_spmd.clone.clone.sunk | while | flops 147317040 | bytes 22999700 | solution.py:84
  124.7 12.4 %fusion.47 = (bf16[1280,1,540]{0,2,1:T(8,128)(2,1)S(1)}, bf16[1280,1,540]{0,2,1:T(8,128)(2,1)S(1)}) fusion(s32[1280]{0:T(1024)S(1)} %get-tuple-element.310, f32[1280]{0:T(1024)S(1)} %get-tuple-element.281, f32[1280]{0:T(1024)S(1)} %get-tuple-element.282, f32[1280]{0:T(1024)S(1)} %reduce.4, f32[1280]{0:T(1024)S(1)} %reduce.5), kind=kLoop, calls=%fused_computation.12.clone.1 | loop fusion | flops 13132800 | bytes 2790400 | tf_op jit(solution)/shard_map/convert
  137.4 7.3 %copy.40 = bf16[1280,2,540]{2,1,0:T(2,128)(2,1)} copy(bf16[1280,2,540]{0,2,1:T(8,128)(2,1)S(1)} %pad_maximum_fusion.2) | data formatting | bytes 5529600 | tf_op jit(solution)/shard_map/while/body/eval_jaxpr/stack | solution.py:74
  144.7 6.6 %convert_element_type.80 = bf16[2560,540]{1,0:T(8,128)(2,1)S(1)} reshape(bf16[1280,2,540]{2,1,0:T(2,128)(2,1)} %copy.40) | data formatting | bytes 5529600 | tf_op jit(solution)/shard_map/while/body/eval_jaxpr/convert_element_type | solution.py:75
  154.9 12.4 %fusion.47 = (bf16[1280,1,540]{0,2,1:T(8,128)(2,1)S(1)}, bf16[1280,1,540]{0,2,1:T(8,128)(2,1)S(1)}) fusion(s32[1280]{0:T(1024)S(1)} %get-tuple-element.310, f32[1280]{0:T(1024)S(1)} %get-tuple-element.281, f32[1280]{0:T(1024)S(1)} %get-tuple-element.282, f32[1280]{0:T(1024)S(1)} %reduce.4, f32[1280]{0:T(1024)S(1)} %reduce.5), kind=kLoop, calls=%fused_computation.12.clone.1 | loop fusion | flops 13132800 | bytes 2790400 | tf_op jit(solution)/shard_map/convert
  167.6 7.3 %copy.40 = bf16[1280,2,540]{2,1,0:T(2,128)(2,1)} copy(bf16[1280,2,540]{0,2,1:T(8,128)(2,1)S(1)} %pad_maximum_fusion.2) | data formatting | bytes 5529600 | tf_op jit(solution)/shard_map/while/body/eval_jaxpr/stack | solution.py:74
  174.9 6.6 %convert_element_type.80 = bf16[2560,540]{1,0:T(8,128)(2,1)S(1)} reshape(bf16[1280,2,540]{2,1,0:T(2,128)(2,1)} %copy.40) | data formatting | bytes 5529600 | tf_op jit(solution)/shard_map/while/body/eval_jaxpr/convert_element_type | solution.py:75
  185.1 12.4 %fusion.47 = (bf16[1280,1,540]{0,2,1:T(8,128)(2,1)S(1)}, bf16[1280,1,540]{0,2,1:T(8,128)(2,1)S(1)}) fusion(s32[1280]{0:T(1024)S(1)} %get-tuple-element.310, f32[1280]{0:T(1024)S(1)} %get-tuple-element.281, f32[1280]{0:T(1024)S(1)} %get-tuple-element.282, f32[1280]{0:T(1024)S(1)} %reduce.4, f32[1280]{0:T(1024)S(1)} %reduce.5), kind=kLoop, calls=%fused_computation.12.clone.1 | loop fusion | flops 13132800 | bytes 2790400 | tf_op jit(solution)/shard_map/convert
  197.8 7.3 %copy.40 = bf16[1280,2,540]{2,1,0:T(2,128)(2,1)} copy(bf16[1280,2,540]{0,2,1:T(8,128)(2,1)S(1)} %pad_maximum_fusion.2) | data formatting | bytes 5529600 | tf_op jit(solution)/shard_map/while/body/eval_jaxpr/stack | solution.py:74
  205.1 6.6 %convert_element_type.80 = bf16[2560,540]{1,0:T(8,128)(2,1)S(1)} reshape(bf16[1280,2,540]{2,1,0:T(2,128)(2,1)} %copy.40) | data formatting | bytes 5529600 | tf_op jit(solution)/shard_map/while/body/eval_jaxpr/convert_element_type | solution.py:75
  215.3 12.4 %fusion.47 = (bf16[1280,1,540]{0,2,1:T(8,128)(2,1)S(1)}, bf16[1280,1,540]{0,2,1:T(8,128)(2,1)S(1)}) fusion(s32[1280]{0:T(1024)S(1)} %get-tuple-element.310, f32[1280]{0:T(1024)S(1)} %get-tuple-element.281, f32[1280]{0:T(1024)S(1)} %get-tuple-element.282, f32[1280]{0:T(1024)S(1)} %reduce.4, f32[1280]{0:T(1024)S(1)} %reduce.5), kind=kLoop, calls=%fused_computation.12.clone.1 | loop fusion | flops 13132800 | bytes 2790400 | tf_op jit(solution)/shard_map/convert
  228.0 7.3 %copy.40 = bf16[1280,2,540]{2,1,0:T(2,128)(2,1)} copy(bf16[1280,2,540]{0,2,1:T(8,128)(2,1)S(1)} %pad_maximum_fusion.2) | data formatting | bytes 5529600 | tf_op jit(solution)/shard_map/while/body/eval_jaxpr/stack | solution.py:74
  235.3 6.6 %convert_element_type.80 = bf16[2560,540]{1,0:T(8,128)(2,1)S(1)} reshape(bf16[1280,2,540]{2,1,0:T(2,128)(2,1)} %copy.40) | data formatting | bytes 5529600 | tf_op jit(solution)/shard_map/while/body/eval_jaxpr/convert_element_type | solution.py:75
  245.6 12.4 %fusion.47 = (bf16[1280,1,540]{0,2,1:T(8,128)(2,1)S(1)}, bf16[1280,1,540]{0,2,1:T(8,128)(2,1)S(1)}) fusion(s32[1280]{0:T(1024)S(1)} %get-tuple-element.310, f32[1280]{0:T(1024)S(1)} %get-tuple-element.281, f32[1280]{0:T(1024)S(1)} %get-tuple-element.282, f32[1280]{0:T(1024)S(1)} %reduce.4, f32[1280]{0:T(1024)S(1)} %reduce.5), kind=kLoop, calls=%fused_computation.12.clone.1 | loop fusion | flops 13132800 | bytes 2790400 | tf_op jit(solution)/shard_map/convert
  258.2 7.3 %copy.40 = bf16[1280,2,540]{2,1,0:T(2,128)(2,1)} copy(bf16[1280,2,540]{0,2,1:T(8,128)(2,1)S(1)} %pad_maximum_fusion.2) | data formatting | bytes 5529600 | tf_op jit(solution)/shard_map/while/body/eval_jaxpr/stack | solution.py:74
  265.5 6.6 %convert_element_type.80 = bf16[2560,540]{1,0:T(8,128)(2,1)S(1)} reshape(bf16[1280,2,540]{2,1,0:T(2,128)(2,1)} %copy.40) | data formatting | bytes 5529600 | tf_op jit(solution)/shard_map/while/body/eval_jaxpr/convert_element_type | solution.py:75
  275.8 12.4 %fusion.47 = (bf16[1280,1,540]{0,2,1:T(8,128)(2,1)S(1)}, bf16[1280,1,540]{0,2,1:T(8,128)(2,1)S(1)}) fusion(s32[1280]{0:T(1024)S(1)} %get-tuple-element.310, f32[1280]{0:T(1024)S(1)} %get-tuple-element.281, f32[1280]{0:T(1024)S(1)} %get-tuple-element.282, f32[1280]{0:T(1024)S(1)} %reduce.4, f32[1280]{0:T(1024)S(1)} %reduce.5), kind=kLoop, calls=%fused_computation.12.clone.1 | loop fusion | flops 13132800 | bytes 2790400 | tf_op jit(solution)/shard_map/convert
  288.4 7.3 %copy.40 = bf16[1280,2,540]{2,1,0:T(2,128)(2,1)} copy(bf16[1280,2,540]{0,2,1:T(8,128)(2,1)S(1)} %pad_maximum_fusion.2) | data formatting | bytes 5529600 | tf_op jit(solution)/shard_map/while/body/eval_jaxpr/stack | solution.py:74
  295.7 6.6 %convert_element_type.80 = bf16[2560,540]{1,0:T(8,128)(2,1)S(1)} reshape(bf16[1280,2,540]{2,1,0:T(2,128)(2,1)} %copy.40) | data formatting | bytes 5529600 | tf_op jit(solution)/shard_map/while/body/eval_jaxpr/convert_element_type | solution.py:75
  306.0 12.4 %fusion.47 = (bf16[1280,1,540]{0,2,1:T(8,128)(2,1)S(1)}, bf16[1280,1,540]{0,2,1:T(8,128)(2,1)S(1)}) fusion(s32[1280]{0:T(1024)S(1)} %get-tuple-element.310, f32[1280]{0:T(1024)S(1)} %get-tuple-element.281, f32[1280]{0:T(1024)S(1)} %get-tuple-element.282, f32[1280]{0:T(1024)S(1)} %reduce.4, f32[1280]{0:T(1024)S(1)} %reduce.5), kind=kLoop, calls=%fused_computation.12.clone.1 | loop fusion | flops 13132800 | bytes 2790400 | tf_op jit(solution)/shard_map/convert
  318.6 7.3 %copy.40 = bf16[1280,2,540]{2,1,0:T(2,128)(2,1)} copy(bf16[1280,2,540]{0,2,1:T(8,128)(2,1)S(1)} %pad_maximum_fusion.2) | data formatting | bytes 5529600 | tf_op jit(solution)/shard_map/while/body/eval_jaxpr/stack | solution.py:74
  325.9 6.6 %convert_element_type.80 = bf16[2560,540]{1,0:T(8,128)(2,1)S(1)} reshape(bf16[1280,2,540]{2,1,0:T(2,128)(2,1)} %copy.40) | data formatting | bytes 5529600 | tf_op jit(solution)/shard_map/while/body/eval_jaxpr/convert_element_type | solution.py:75
  336.2 12.4 %fusion.47 = (bf16[1280,1,540]{0,2,1:T(8,128)(2,1)S(1)}, bf16[1280,1,540]{0,2,1:T(8,128)(2,1)S(1)}) fusion(s32[1280]{0:T(1024)S(1)} %get-tuple-element.310, f32[1280]{0:T(1024)S(1)} %get-tuple-element.281, f32[1280]{0:T(1024)S(1)} %get-tuple-element.282, f32[1280]{0:T(1024)S(1)} %reduce.4, f32[1280]{0:T(1024)S(1)} %reduce.5), kind=kLoop, calls=%fused_computation.12.clone.1 | loop fusion | flops 13132800 | bytes 2790400 | tf_op jit(solution)/shard_map/convert
  348.9 7.3 %copy.40 = bf16[1280,2,540]{2,1,0:T(2,128)(2,1)} copy(bf16[1280,2,540]{0,2,1:T(8,128)(2,1)S(1)} %pad_maximum_fusion.2) | data formatting | bytes 5529600 | tf_op jit(solution)/shard_map/while/body/eval_jaxpr/stack | solution.py:74
  356.1 6.6 %convert_element_type.80 = bf16[2560,540]{1,0:T(8,128)(2,1)S(1)} reshape(bf16[1280,2,540]{2,1,0:T(2,128)(2,1)} %copy.40) | data formatting | bytes 5529600 | tf_op jit(solution)/shard_map/while/body/eval_jaxpr/convert_element_type | solution.py:75
  366.2 16.6 %all_gather.6 = f32[4,2,4,4320]{3,2,1,0:T(4,128)S(1)} all-gather(f32[1,2,4,4320]{3,2,1,0:T(4,128)S(1)} %all_gather_reshape.3), channel_id=1, replica_groups=mesh['wave'=4,'lev'=4,'cpl'=2] {'lev'}, dimensions={0}, use_global_device_ids=true | all-gather | bytes 691200 | tf_op jit(solution)/shard_map/all_gather | solution.py:90
  383.8 24.6 %all-gather.2.cloned.1.call-done = f32[16,4,4320]{2,1,0:T(4,128)} async-done(((f32[2,4,4320]{2,1,0:T(4,128)}), f32[16,4,4320]{2,1,0:T(4,128)}) %all-gather.2.cloned.1.call-update) | async-done | bytes 1105936 | tf_op jit(solution)/shard_map/all_gather | solution.py:91
  (114 shorter events, 42.3 us)
Async XLA Ops:
  60.9 52.4 %copy-start = (s32[1280]{0:T(1024)S(1)}, s32[1280]{0:T(1024)}, u32[]{:S(2)}) copy-start(s32[1280]{0:T(1024)} %param.12) | copy-start | bytes 15364
  109.0 10.6 %all-to-all-start = ((bf16[320,8,48]{0,2,1:T(8,128)(2,1)}), bf16[320,8,48]{0,2,1:T(8,128)(2,1)S(1)}, u32[]{:S(2)}, u32[]{:S(2)}) async-start(bf16[320,8,48]{0,2,1:T(8,128)(2,1)} %copy.25), calls=%async_computation | async-start | bytes 589824 | tf_op jit(solution)/shard_map/all_to_all | solution.py:52
  113.3 295.1 %all-gather.2.cloned.1.call-start = ((), (), s32[]{:S(2)}) async-start(), calls=%async_computation.1 | async-start | bytes 1253376 | tf_op jit(solution)/shard_map/all_gather | solution.py:91
  113.3 10.1 %copy-start.1 = (f32[6]{0:T(128)S(1)}, f32[6]{0:T(128)}, u32[]{:S(2)}) copy-start(f32[6]{0:T(128)} %param.13) | copy-start | bytes 76
  123.4 260.2 %copy-start.2 = (f32[16]{0:T(128)S(1)}, f32[16]{0:T(128)}, u32[]{:S(2)}) copy-start(f32[16]{0:T(128)} %param.15) | copy-start | bytes 196
  123.4 260.3 %copy-start.3 = (s32[16]{0:T(128)S(1)}, s32[16]{0:T(128)}, u32[]{:S(2)}) copy-start(s32[16]{0:T(128)} %param.14) | copy-start | bytes 196
Sparse Core Ops, SparseCore 0:
  383.7 24.5 all-gather.1
